TPU v7x, 32 devices: a whole 2x2x4 slice. The times are simulated.
32 devices in a mesh: bucket: 4 (over y, x), group: 8 (over z, core).
Axes of the slice: x: 2, y: 2, z: 4, core: 2. Of those that a mesh axis runs over, the one named last changes fastest.
Arguments:
- embeddings: bfloat16 [4, 8, 4, 128, 768], P('bucket', 'group'), may hold values from -6 to 6
- counts: int32 [4, 8, 4, 1], P('bucket', 'group'), may hold values from 42 to 128, as said below
Outputs:
- neighbour_sums: bfloat16 [4, 8, 512, 768], P('bucket', 'group')
Inputs may be any that keep to these rules, and one draw needn't show every extreme that they name: `counts`: each count is a live prefix of its 128 slots; in every draw some slot range is full.
All inputs are finite; a program needn't handle non-finite values.
Results may differ from a plain program's by a relative error of at most 0.0052.
Values may be sent and summed in bfloat16 or wider, within the bound.
No kernel may reach another device: no remote copies, remote signals or barrier semaphores. Data moves between devices by JAX's collectives and lax.ppermute only.
A program may use at most 128 MiB of HBM per device.

v0:
```python
import jax
import jax.numpy as jnp
from jax import lax
from jax.sharding import PartitionSpec as P

ROUNDS = 4
EPS = 1e-06
TEMP = 12.0


def normalize(block):
    values = block.astype(jnp.float32)
    return (values * lax.rsqrt(jnp.sum(values * values, axis=-1, keepdims=True) + EPS)).astype(
        jnp.bfloat16
    )


def weigh(unit_a, unit_b, live_b, extra):
    scores = jnp.dot(unit_a, unit_b.T, preferred_element_type=jnp.float32)
    return jnp.exp(TEMP * scores) * live_b[None, :] * extra


def per_device(embeddings, counts):
    slabs, slab_counts = (
        lax.all_to_all(embeddings, "bucket", split_axis=2, concat_axis=0, tiled=True),
        lax.all_to_all(counts, "bucket", split_axis=2, concat_axis=0, tiled=True),
    )
    sources = slabs.shape[0]
    slot_rows = slabs.shape[3]
    width = slabs.shape[4]
    rows = sources * slot_rows
    data = slabs.reshape(rows, width)
    slot_index = lax.broadcasted_iota(jnp.int32, (sources, slot_rows), 1)
    live = (slot_index < slab_counts.reshape(sources, 1)).astype(jnp.float32).reshape(rows)
    marks = live.astype(jnp.bfloat16)
    unit = normalize(data)
    not_self = 1.0 - jnp.eye(rows, dtype=jnp.float32)
    own = weigh(unit, unit, live, not_self)
    summed = jnp.dot(own.astype(jnp.bfloat16), data, preferred_element_type=jnp.float32)
    squares = jnp.sum(own * own, axis=1)
    all_data, all_marks = (
        lax.all_gather(data, "group", axis=0, tiled=True),
        lax.all_gather(marks, "group", axis=0, tiled=True),
    )
    blocks = lax.axis_size("group")
    position = lax.axis_index("group")
    for dist in range(1, ROUNDS + 1):
        for sign in (1, -1):
            other = (position + sign * dist) % blocks
            start = other * rows
            got_data = lax.dynamic_slice_in_dim(all_data, start, rows, 0)
            got_live = lax.dynamic_slice_in_dim(all_marks, start, rows, 0).astype(jnp.float32)
            weights = weigh(unit, normalize(got_data), got_live, 1.0)
            summed = summed + jnp.dot(
                weights.astype(jnp.bfloat16), got_data, preferred_element_type=jnp.float32
            )
            squares = squares + jnp.sum(weights * weights, axis=1)
    result = summed * lax.rsqrt(squares)[:, None] * live[:, None]
    return result.astype(jnp.bfloat16).reshape(1, 1, rows, width)


def solution(mesh):
    in_specs = (P("bucket", "group", None, None, None), P("bucket", "group", None, None))
    out_specs = P("bucket", "group", None, None)
    return jax.shard_map(
        per_device, mesh=mesh, in_specs=in_specs, out_specs=out_specs, check_vma=False
    )
```

profile of v0, /device:TPU:0, one launch (start us, length us, event | category | flops | bytes accessed | tf_op | source)
XLA Modules:
  0.0 112.1 jit_solution(2783596257850077988)
XLA Ops:
  6.5 17.3 %all_to_all.8 = bf16[1,1,4,128,768]{4,3,1,0,2:T(8,128)(2,1)} all-to-all(bf16[1,1,4,128,768]{4,3,1,0,2:T(8,128)(2,1)} %bitcast.36), channel_id=1, replica_groups=mesh['bucket'=4,'group'=8] {'bucket'}, dimensions={2} | all-to-all | bytes 1572864 | tf_op jit(solution)/shard_map/all_to_all | solution.py:25
  23.9 0.7 copy.6
  24.5 3.2 %all-to-all-start.1 = ((s32[1,1,4,1]{3,1,0,2:T(1,128)}), s32[1,1,4,1]{3,1,0,2:T(1,128)S(1)}, u32[]{:S(2)}, u32[]{:S(2)}) async-start(s32[1,1,4,1]{3,1,0,2:T(1,128)} %copy.6), calls=%async_computation.1 | async-start | bytes 4096 | tf_op jit(solution)/shard_map/all_to_all | solution.py:26
  27.9 4.4 %all-to-all-done.1 = s32[1,1,4,1]{3,1,0,2:T(1,128)S(1)} async-done(((s32[1,1,4,1]{3,1,0,2:T(1,128)}), s32[1,1,4,1]{3,1,0,2:T(1,128)S(1)}, u32[]{:S(2)}, u32[]{:S(2)}) %all-to-all-start.1) | async-done | bytes 48 | tf_op jit(solution)/shard_map/all_to_all | solution.py:26
  32.6 13.6 %all-gather = bf16[8,1,512]{2,1,0:T(2,128)(2,1)S(1)} all-gather(bf16[1,1,512]{2,1,0:T(2,128)(2,1)S(1)} %reshape.165), channel_id=1, replica_groups=mesh['bucket'=4,'group'=8] {'group'}, dimensions={0}, use_global_device_ids=true | all-gather | bytes 9216 | tf_op jit(solution)/shard_map/all_gather | solution.py:43
  47.0 0.7 multiply_reduce_fusion.8
  48.4 40.3 %all-gather.3.cloned.1.call-done = bf16[4096,768]{1,0:T(8,128)(2,1)} async-done(((bf16[512,768]{1,0:T(8,128)(2,1)}), bf16[4096,768]{1,0:T(8,128)(2,1)}) %all-gather.3.cloned.1.call-update) | async-done | bytes 6291472 | tf_op jit(solution)/shard_map/all_gather | solution.py:42
  88.6 4.2 %fusion.16 = (f32[512]{0:T(512)S(1)}, f32[512]{0:T(512)S(1)}, f32[512]{0:T(512)S(1)}, f32[512]{0:T(512)S(1)}, f32[512]{0:T(512)S(1)}, /*index=5*/f32[512]{0:T(512)S(1)}, f32[512]{0:T(512)S(1)}, f32[512]{0:T(512)S(1)}) fusion(bf16[4096,768]{1,0:T(8,128)(2,1)} %all-gather.3.cloned.1.call-done, s32[]{:T(128)S(6)} %select_n.82, s32[]{:T(128)S(6)} %select_n.80, ...), kind=kLoop, calls=%fused_computation.34 | loop fusion | flops 9433088 | bytes 6307872 | tf_op jit(solution)/shard_map/reduce_sum | solution.py:13
  93.3 0.7 multiply_reduce_fusion.1
  94.0 0.7 multiply_reduce_fusion.2
  94.8 0.7 multiply_reduce_fusion.3
  95.5 0.7 multiply_reduce_fusion.4
  96.2 0.7 multiply_reduce_fusion.5
  97.0 0.7 multiply_reduce_fusion.6
  97.7 0.7 multiply_reduce_fusion.7
  98.4 0.7 multiply_reduce_fusion
  99.2 0.6 fusion.57
  99.8 0.6 fusion.60
  100.4 0.6 fusion.63
  101.0 0.6 fusion.66
  101.6 0.6 fusion.69
  102.2 0.6 fusion.72
  102.8 0.6 fusion.75
  103.4 1.8 %fusion.37 = bf16[1,1,512,768]{3,2,1,0:T(8,128)(2,1)} fusion(f32[512,768]{1,0:T(8,128)S(1)} %fusion.57, f32[512,768]{1,0:T(8,128)S(1)} %fusion.60, f32[512,768]{1,0:T(8,128)S(1)} %fusion.63, f32[512,768]{1,0:T(8,128)S(1)} %fusion.66, f32[512,768]{1,0:T(8,128)S(1)} %fusion.69, f32[512,768]{1,0:T(8,128)S(1)} %fusion.72, f32[512,768]{1,0:T(8,128)S(1)} %fusion.85, ...), kind=kOutput, calls=%fused_computation.66 | convolution fusion | flops 406978560 | bytes 14684164 | tf_op jit(solution)/shard_map/dot_general | solution.py:54
  (24 shorter events, 2.1 us)
Async XLA Ops:
  6.5 17.3 %copy-start.2 = (s32[1,1,4,1]{2,3,1,0:T(1,128)S(1)}, s32[1,1,4,1]{2,3,1,0:T(1,128)}, u32[]{:S(2)}) copy-start(s32[1,1,4,1]{2,3,1,0:T(1,128)} %param.3) | copy-start | bytes 52
  6.5 82.1 %all-gather.3.cloned.1.call-start = ((), (), s32[]{:S(2)}) async-start(), calls=%async_computation.2 | async-start | bytes 7077888 | tf_op jit(solution)/shard_map/all_gather | solution.py:42
  23.8 22.5 %copy-start = (bf16[1,1,4,128,768]{4,3,1,0,2:T(8,128)(2,1)S(1)}, bf16[1,1,4,128,768]{4,3,1,0,2:T(8,128)(2,1)}, u32[]{:S(2)}) copy-start(bf16[1,1,4,128,768]{4,3,1,0,2:T(8,128)(2,1)} %all_to_all.8) | copy-start | bytes 2359300
  24.5 7.8 %all-to-all-start.1 = ((s32[1,1,4,1]{3,1,0,2:T(1,128)}), s32[1,1,4,1]{3,1,0,2:T(1,128)S(1)}, u32[]{:S(2)}, u32[]{:S(2)}) async-start(s32[1,1,4,1]{3,1,0,2:T(1,128)} %copy.6), calls=%async_computation.1 | async-start | bytes 4096 | tf_op jit(solution)/shard_map/all_to_all | solution.py:26
  88.6 4.7 %copy-start.1 = (bf16[4096,768]{1,0:T(8,128)(2,1)S(1)}, bf16[4096,768]{1,0:T(8,128)(2,1)}, u32[]{:S(2)}) copy-start(bf16[4096,768]{1,0:T(8,128)(2,1)} %all-gather.3.cloned.1.call-done) | copy-start | bytes 18874372
Sparse Core Ops, SparseCore 0:
  24.0 64.6 all-gather.2
where the time goes:
time: 112 us
  waiting for transfers between devices  44.7 us (40%)
  blocking collectives  30.9 us (28%)
  between operations  13.7 us (12%)
  matrix products  13.2 us (12%)
  other arithmetic  5.33 us (5%)
  starting transfers between devices  3.22 us (3%)
    all_gather x1, waiting for transfers between devices, per_device(): lax.all_gather(data, 'group', axis=0, tiled=True)  40.3 us
    all_to_all x1, blocking collectives, per_device(): lax.all_to_all(embeddings, 'bucket', split_axis=2, concat_axis=0, tiled=T...  17.3 us
    all_gather x1, blocking collectives, per_device(): lax.all_gather(marks, 'group', axis=0, tiled=True)  13.6 us
    dot_general x9, matrix products, weigh(): scores = jnp.dot(unit_a, unit_b.T, preferred_element_type=jnp.float32)  6.57 us
    dot_general x8, matrix products, per_device(): jnp.dot(weights.astype(jnp.bfloat16), got_data, preferred_element_type=jn...  6.04 us
    reduce_sum x2, other arithmetic, normalize(): jnp.sum(values * values, axis=-1, keepdims=True) + EPS  4.47 us
    all_to_all x1, waiting for transfers between devices, per_device(): lax.all_to_all(counts, 'bucket', split_axis=2, concat_axis=0, tiled=True)  4.43 us
    all_to_all x1, starting transfers between devices, per_device(): lax.all_to_all(counts, 'bucket', split_axis=2, concat_axis=0, tiled=True)  3.22 us
  transfers between devices with their start and end apart: 2, of which 2 were waited for; matrix products, arithmetic and copies ran while one was open for 3% of the time, Pallas kernels for 0%

commit v1 on v0

--- a/solution.py
+++ b/solution.py
@@ -6,6 +6,25 @@
 ROUNDS = 4
 EPS = 1e-06
 TEMP = 12.0
+
+
+def define_the_units(page):
+    arr_out = jax.lax.axis_size("group")
+    low = jax.lax.axis_index("group")
+    later, y2, new = (arr_out, low, page.shape[0])
+    buffer = [(ix, (ix + 1) % later) for ix in range(later)]
+    pieces_in = [(ix, (ix - 1) % later) for ix in range(later)]
+    outer = jnp.zeros((*page.shape[:0], later * new, *page.shape[1:]), page.dtype)
+    outer = lax.dynamic_update_slice_in_dim(outer, page, y2 * new, axis=0)
+    newest = spare = page
+    front = later // 2
+    for jj in [*range(1, front + 1)]:
+        newest = jax.lax.ppermute(newest, "group", buffer)
+        outer = lax.dynamic_update_slice_in_dim(outer, newest, (y2 - jj) % later * new, axis=0)
+        if jj < later - front:
+            spare = jax.lax.ppermute(spare, "group", pieces_in)
+            outer = lax.dynamic_update_slice_in_dim(outer, spare, (y2 + jj) % later * new, axis=0)
+    return outer
 
 
 def normalize(block):
@@ -39,7 +58,7 @@
     summed = jnp.dot(own.astype(jnp.bfloat16), data, preferred_element_type=jnp.float32)
     squares = jnp.sum(own * own, axis=1)
     all_data, all_marks = (
-        lax.all_gather(data, "group", axis=0, tiled=True),
+        define_the_units(data),
         lax.all_gather(marks, "group", axis=0, tiled=True),
     )
     blocks = lax.axis_size("group")

time: 112 us -> 107 us (0.955)
  between operations: 13.7 us -> 0.36 us
  blocking collectives: 30.9 us -> 40 us
  starting transfers between devices: 3.22 us -> 11.3 us
  waiting for transfers between devices: 44.7 us -> 37.6 us
  other arithmetic: 5.33 us -> 2.41 us
    all_gather x1 -> x0, waiting for transfers between devices: 40.3 us -> none  [per_device(): lax.all_gather(data, 'group', axis=0, tiled=True)]
    ppermute x0 -> x7, waiting for transfers between devices: none -> 33.1 us  [the longest x3 30.9 us: define_the_units(): spare = jax.lax.ppermute(spare, 'group', pieces_in)]
    all_gather x1, blocking collectives: 13.6 us -> 23.4 us  [per_device(): lax.all_gather(marks, 'group', axis=0, tiled=True)]
    ppermute x0 -> x7, starting transfers between devices: none -> 8.11 us  [the longest x3 7.86 us: define_the_units(): spare = jax.lax.ppermute(spare, 'group', pieces_in)]
    reduce_sum x2, other arithmetic: 4.47 us -> 1.56 us  [normalize(): jnp.sum(values * values, axis=-1, keepdims=True) + EPS]
  transfers between devices with their start and end apart: 2 -> 8, of which waited for: 2 -> 4; matrix products, arithmetic and copies ran while one was open for 3% -> 4% of each run, Pallas kernels for 0% -> 0%
where the time goes in v1:
time: 107 us
  blocking collectives  40 us (37%)
  waiting for transfers between devices  37.6 us (35%)
  matrix products  13.4 us (13%)
  starting transfers between devices  11.3 us (11%)
  other arithmetic  2.41 us (2%)
  local copies, waits for them, and re-layouts  1.59 us (1%)
    ppermute x3, waiting for transfers between devices, define_the_units(): spare = jax.lax.ppermute(spare, 'group', pieces_in)  30.9 us
    all_gather x1, blocking collectives, per_device(): lax.all_gather(marks, 'group', axis=0, tiled=True)  23.4 us
    all_to_all x1, blocking collectives, per_device(): lax.all_to_all(embeddings, 'bucket', split_axis=2, concat_axis=0, tiled=T...  16.7 us
    ppermute x3, starting transfers between devices, define_the_units(): spare = jax.lax.ppermute(spare, 'group', pieces_in)  7.86 us
    dot_general x9, matrix products, weigh(): scores = jnp.dot(unit_a, unit_b.T, preferred_element_type=jnp.float32)  6.57 us
    dot_general x8, matrix products, per_device(): jnp.dot(weights.astype(jnp.bfloat16), got_data, preferred_element_type=jn...  6.27 us
    all_to_all x1, waiting for transfers between devices, per_device(): lax.all_to_all(counts, 'bucket', split_axis=2, concat_axis=0, tiled=True)  4.42 us
    all_to_all x1, starting transfers between devices, per_device(): lax.all_to_all(counts, 'bucket', split_axis=2, concat_axis=0, tiled=True)  3.22 us
  transfers between devices with their start and end apart: 8, of which 4 were waited for; matrix products, arithmetic and copies ran while one was open for 4% of the time, Pallas kernels for 0%

profile of v1, /device:TPU:0, one launch (start us, length us, event | category | flops | bytes accessed | tf_op | source)
XLA Modules:
  0.0 106.7 jit_solution(9111560680733446689)
XLA Ops:
  0.0 16.7 %all_to_all.8 = bf16[1,1,4,128,768]{4,3,1,0,2:T(8,128)(2,1)S(1)} all-to-all(bf16[1,1,4,128,768]{4,3,1,0,2:T(8,128)(2,1)} %bitcast.38), channel_id=1, replica_groups=mesh['bucket'=4,'group'=8] {'bucket'}, dimensions={2} | all-to-all | bytes 1572864 | tf_op jit(solution)/shard_map/all_to_all | solution.py:44
  16.7 0.7 copy.6
  17.3 3.2 %all-to-all-start.1 = ((s32[1,1,4,1]{3,1,0,2:T(1,128)}), s32[1,1,4,1]{3,1,0,2:T(1,128)S(1)}, u32[]{:S(2)}, u32[]{:S(2)}) async-start(s32[1,1,4,1]{3,1,0,2:T(1,128)} %copy.6), calls=%async_computation.1 | async-start | bytes 4096 | tf_op jit(solution)/shard_map/all_to_all | solution.py:45
  20.7 4.4 %all-to-all-done.1 = s32[1,1,4,1]{3,1,0,2:T(1,128)S(1)} async-done(((s32[1,1,4,1]{3,1,0,2:T(1,128)}), s32[1,1,4,1]{3,1,0,2:T(1,128)S(1)}, u32[]{:S(2)}, u32[]{:S(2)}) %all-to-all-start.1) | async-done | bytes 48 | tf_op jit(solution)/shard_map/all_to_all | solution.py:45
  25.3 2.4 %collective-permute-start.1 = (bf16[512,768]{1,0:T(8,128)(2,1)S(1)}, bf16[512,768]{1,0:T(8,128)(2,1)S(1)}, u32[]{:S(2)}, u32[]{:S(2)}) collective-permute-start(bf16[512,768]{1,0:T(8,128)(2,1)S(1)} %bitcast.35), channel_id=1, source_target_pairs={{0,7},{1,0},{2,1},{3,2},{4,3},{5,4},{6,5},{7,6},{8,15},{9,8},{10,9... | collective-permute-start | bytes 2359304 | tf_op jit(solution)/shard_map/ppermute | solution.py:25
  27.7 2.2 %collective-permute-done = bf16[512,768]{1,0:T(8,128)(2,1)S(1)} collective-permute-done((bf16[512,768]{1,0:T(8,128)(2,1)S(1)}, bf16[512,768]{1,0:T(8,128)(2,1)S(1)}, u32[]{:S(2)}, u32[]{:S(2)}) %collective-permute-start) | collective-permute-done | bytes 786464 | tf_op jit(solution)/shard_map/ppermute | solution.py:22
  30.0 23.4 %all-gather = bf16[8,1,512]{2,1,0:T(2,128)(2,1)S(1)} all-gather(bf16[1,1,512]{2,1,0:T(2,128)(2,1)S(1)} %reshape.165), channel_id=1, replica_groups=mesh['bucket'=4,'group'=8] {'group'}, dimensions={0}, use_global_device_ids=true | all-gather | bytes 9216 | tf_op jit(solution)/shard_map/all_gather | solution.py:62
  54.0 1.7 %collective-permute-start.3 = (bf16[512,768]{1,0:T(8,128)(2,1)S(1)}, bf16[512,768]{1,0:T(8,128)(2,1)S(1)}, u32[]{:S(2)}, u32[]{:S(2)}) collective-permute-start(bf16[512,768]{1,0:T(8,128)(2,1)S(1)} %collective-permute-done.1), channel_id=1, source_target_pairs={{0,7},{1,0},{2,1},{3,2},{4,3},{5,4},{6,5},{7,6},{8,15},{9,8},{10,9... | collective-permute-start | bytes 2359304 | tf_op jit(solution)/shard_map/ppermute | solution.py:25
  56.0 0.8 multiply_reduce_fusion.8
  57.3 16.1 %collective-permute-done.3 = bf16[512,768]{1,0:T(8,128)(2,1)S(1)} collective-permute-done((bf16[512,768]{1,0:T(8,128)(2,1)S(1)}, bf16[512,768]{1,0:T(8,128)(2,1)S(1)}, u32[]{:S(2)}, u32[]{:S(2)}) %collective-permute-start.3) | collective-permute-done | bytes 786464 | tf_op jit(solution)/shard_map/ppermute | solution.py:25
  73.4 3.7 %collective-permute-start.5 = (bf16[512,768]{1,0:T(8,128)(2,1)S(1)}, bf16[512,768]{1,0:T(8,128)(2,1)S(1)}, u32[]{:S(2)}, u32[]{:S(2)}) collective-permute-start(bf16[512,768]{1,0:T(8,128)(2,1)S(1)} %collective-permute-done.3), channel_id=1, source_target_pairs={{0,7},{1,0},{2,1},{3,2},{4,3},{5,4},{6,5},{7,6},{8,15},{9,8},{10,9... | collective-permute-start | bytes 2359304 | tf_op jit(solution)/shard_map/ppermute | solution.py:25
  78.2 14.8 %collective-permute-done.5 = bf16[512,768]{1,0:T(8,128)(2,1)S(1)} collective-permute-done((bf16[512,768]{1,0:T(8,128)(2,1)S(1)}, bf16[512,768]{1,0:T(8,128)(2,1)S(1)}, u32[]{:S(2)}, u32[]{:S(2)}) %collective-permute-start.5) | collective-permute-done | bytes 786464 | tf_op jit(solution)/shard_map/ppermute | solution.py:25
  93.2 1.3 %fusion.2 = (f32[512]{0:T(512)S(1)}, f32[512]{0:T(512)S(1)}, f32[512]{0:T(512)S(1)}, f32[512]{0:T(512)S(1)}, f32[512]{0:T(512)S(1)}, /*index=5*/f32[512]{0:T(512)S(1)}, f32[512]{0:T(512)S(1)}, f32[512]{0:T(512)S(1)}) fusion(bf16[4096,768]{1,0:T(8,128)(2,1)S(1)} %constant_dynamic-update-slice_fusion, s32[]{:T(128)S(6)} %select_n.95, s32[]{:T(128)S(6)} %select_n.105, ...), kind=kLoop, calls=%fused_computation.20 | loop fusion | flops 9433088 | bytes 6307872 | tf_op jit(solution)/shard_map/reduce_sum | solution.py:32
  94.6 0.7 multiply_reduce_fusion.1
  95.9 0.7 multiply_reduce_fusion.2
  97.3 0.7 multiply_reduce_fusion.3
  98.0 0.6 fusion.66
  98.6 0.7 multiply_reduce_fusion.4
  99.9 0.7 multiply_reduce_fusion.5
  101.3 0.7 multiply_reduce_fusion.6
  102.6 0.7 multiply_reduce_fusion.7
  103.3 0.6 fusion.78
  103.9 0.7 multiply_reduce_fusion
  104.7 2.1 %fusion.53 = bf16[1,1,512,768]{3,2,1,0:T(8,128)(2,1)} fusion(f32[512]{0:T(512)S(1)} %get-tuple-element.24, f32[512]{0:T(512)S(1)} %add_rsqrt_fusion, f32[512,768]{1,0:T(8,128)S(1)} %fusion.60, f32[512,768]{1,0:T(8,128)S(1)} %fusion.63, f32[512,768]{1,0:T(8,128)S(1)} %fusion.66, f32[512,768]{1,0:T(8,128)S(1)} %fusion.69, f32[512,768]{1,0:T(8,128)S(1)} %fusion.72, ...), kind=kOutput, calls=%fused_computation.84 | convolution fusion | flops 406978560 | bytes 14684164 | tf_op jit(solution)/shard_map/dot_general | solution.py:73
  (40 shorter events, 5.9 us)
Async XLA Ops:
  0.0 16.7 %copy-start = (s32[1,1,4,1]{2,3,1,0:T(1,128)S(1)}, s32[1,1,4,1]{2,3,1,0:T(1,128)}, u32[]{:S(2)}) copy-start(s32[1,1,4,1]{2,3,1,0:T(1,128)} %param.3) | copy-start | bytes 52
  16.7 13.3 %collective-permute-start = (bf16[512,768]{1,0:T(8,128)(2,1)S(1)}, bf16[512,768]{1,0:T(8,128)(2,1)S(1)}, u32[]{:S(2)}, u32[]{:S(2)}) collective-permute-start(bf16[512,768]{1,0:T(8,128)(2,1)S(1)} %bitcast.34), channel_id=1, source_target_pairs={{0,1},{1,2},{2,3},{3,4},{4,5},{5,6},{6,7},{7,0},{8,9},{9,10},{10,1... | collective-permute-start | bytes 2359304 | tf_op jit(solution)/shard_map/ppermute | solution.py:22
  17.3 7.8 %all-to-all-start.1 = ((s32[1,1,4,1]{3,1,0,2:T(1,128)}), s32[1,1,4,1]{3,1,0,2:T(1,128)S(1)}, u32[]{:S(2)}, u32[]{:S(2)}) async-start(s32[1,1,4,1]{3,1,0,2:T(1,128)} %copy.6), calls=%async_computation.1 | async-start | bytes 4096 | tf_op jit(solution)/shard_map/all_to_all | solution.py:45
  25.3 28.8 %collective-permute-start.1 = (bf16[512,768]{1,0:T(8,128)(2,1)S(1)}, bf16[512,768]{1,0:T(8,128)(2,1)S(1)}, u32[]{:S(2)}, u32[]{:S(2)}) collective-permute-start(bf16[512,768]{1,0:T(8,128)(2,1)S(1)} %bitcast.35), channel_id=1, source_target_pairs={{0,7},{1,0},{2,1},{3,2},{4,3},{5,4},{6,5},{7,6},{8,15},{9,8},{10,9... | collective-permute-start | bytes 2359304 | tf_op jit(solution)/shard_map/ppermute | solution.py:25
  29.9 25.8 %collective-permute-start.2 = (bf16[512,768]{1,0:T(8,128)(2,1)S(1)}, bf16[512,768]{1,0:T(8,128)(2,1)S(1)}, u32[]{:S(2)}, u32[]{:S(2)}) collective-permute-start(bf16[512,768]{1,0:T(8,128)(2,1)S(1)} %collective-permute-done), channel_id=1, source_target_pairs={{0,1},{1,2},{2,3},{3,4},{4,5},{5,6},{6,7},{7,0},{8,9},{9,10},{10,1... | collective-permute-start | bytes 2359304 | tf_op jit(solution)/shard_map/ppermute | solution.py:22
  54.0 19.4 %collective-permute-start.3 = (bf16[512,768]{1,0:T(8,128)(2,1)S(1)}, bf16[512,768]{1,0:T(8,128)(2,1)S(1)}, u32[]{:S(2)}, u32[]{:S(2)}) collective-permute-start(bf16[512,768]{1,0:T(8,128)(2,1)S(1)} %collective-permute-done.1), channel_id=1, source_target_pairs={{0,7},{1,0},{2,1},{3,2},{4,3},{5,4},{6,5},{7,6},{8,15},{9,8},{10,9... | collective-permute-start | bytes 2359304 | tf_op jit(solution)/shard_map/ppermute | solution.py:25
  55.8 21.9 %collective-permute-start.4 = (bf16[512,768]{1,0:T(8,128)(2,1)S(1)}, bf16[512,768]{1,0:T(8,128)(2,1)S(1)}, u32[]{:S(2)}, u32[]{:S(2)}) collective-permute-start(bf16[512,768]{1,0:T(8,128)(2,1)S(1)} %collective-permute-done.2), channel_id=1, source_target_pairs={{0,1},{1,2},{2,3},{3,4},{4,5},{5,6},{6,7},{7,0},{8,9},{9,10},{10,1... | collective-permute-start | bytes 2359304 | tf_op jit(solution)/shard_map/ppermute | solution.py:22
  73.4 19.6 %collective-permute-start.5 = (bf16[512,768]{1,0:T(8,128)(2,1)S(1)}, bf16[512,768]{1,0:T(8,128)(2,1)S(1)}, u32[]{:S(2)}, u32[]{:S(2)}) collective-permute-start(bf16[512,768]{1,0:T(8,128)(2,1)S(1)} %collective-permute-done.3), channel_id=1, source_target_pairs={{0,7},{1,0},{2,1},{3,2},{4,3},{5,4},{6,5},{7,6},{8,15},{9,8},{10,9... | collective-permute-start | bytes 2359304 | tf_op jit(solution)/shard_map/ppermute | solution.py:25
  77.6 15.5 %collective-permute-start.6 = (bf16[512,768]{1,0:T(8,128)(2,1)S(1)}, bf16[512,768]{1,0:T(8,128)(2,1)S(1)}, u32[]{:S(2)}, u32[]{:S(2)}) collective-permute-start(bf16[512,768]{1,0:T(8,128)(2,1)S(1)} %collective-permute-done.4), channel_id=1, source_target_pairs={{0,1},{1,2},{2,3},{3,4},{4,5},{5,6},{6,7},{7,0},{8,9},{9,10},{10,1... | collective-permute-start | bytes 2359304 | tf_op jit(solution)/shard_map/ppermute | solution.py:22
